TPU v7x, 256 devices: a whole 4x4x8 slice. The times are simulated.
256 devices in a mesh: pb: 8 (over y, core), kv: 32 (over z, x).
Axes of the slice: x: 4, y: 4, z: 8, core: 2. Of those that a mesh axis runs over, the one named last changes fastest.
Arguments:
- queries: bfloat16 [65536, 4096], P(('pb', 'kv')), may hold values from -6 to 6
- keys: bfloat16 [8192, 4096], P(('pb', 'kv')), may hold values from -6 to 6
- values: bfloat16 [8192, 4096], P(('pb', 'kv')), may hold values from -6 to 6
- key_lists: int32 [512, 8], P('pb'), may hold values from 0 to 63, as said below
- counts: int32 [512], P('pb'), may hold values from 1 to 8, as said below
Outputs:
- attended: bfloat16 [65536, 4096], P(('pb', 'kv'))
Inputs may be any that keep to these rules, and one draw needn't show every extreme that they name: For every query block the first counts entries of its row of key_lists name different key blocks; entries past counts are valid block numbers that do not take part. `counts`: some query block uses all 8 entries of its list.
All inputs are finite; a program needn't handle non-finite values.
Results may differ from a plain program's by a relative error of at most 0.011.
Values may be sent and summed in bfloat16 or wider, within the bound.
No kernel may reach another device: no remote copies, remote signals or barrier semaphores. Data moves between devices by JAX's collectives and lax.ppermute only.
A program may use at most 64 MiB of HBM per device.

v0:
```python
import math
import jax
import jax.numpy as jnp
from jax import lax
from jax.sharding import PartitionSpec as P

HEADS = 32
HD = 128
BLK = 128
MOST = 8


def regroup(split_array, kv_count, pb_count):
    tokens_each = split_array.shape[0] // (kv_count * pb_count)
    shaped = split_array.reshape(kv_count, pb_count, tokens_each, split_array.shape[1])
    return shaped.transpose(1, 0, 2, 3).reshape(-1, split_array.shape[1])


def per_device(queries, keys, values, key_lists, counts):
    kv_count = lax.axis_size("kv")
    pb_count = lax.axis_size("pb")
    head_local = HEADS // kv_count
    scaling = HD ** (-0.5)
    key_whole, value_whole = (
        lax.all_gather(keys, "pb", axis=0, tiled=True),
        lax.all_gather(values, "pb", axis=0, tiled=True),
    )
    key_split, value_split = (
        lax.all_to_all(key_whole, "kv", split_axis=1, concat_axis=0, tiled=True),
        lax.all_to_all(value_whole, "kv", split_axis=1, concat_axis=0, tiled=True),
    )
    key_heads = regroup(key_split, kv_count, pb_count)
    value_heads = regroup(value_split, kv_count, pb_count)
    key_blocks = key_heads.reshape(-1, BLK, head_local, HD)
    value_blocks = value_heads.reshape(-1, BLK, head_local, HD)
    slot_of_key = jnp.arange(MOST * BLK, dtype=jnp.int32) // BLK

    def padded_group(item):
        group_queries, group_lists, group_counts = item
        members = group_queries.shape[0]
        listed_keys = key_blocks[group_lists].reshape(members, MOST * BLK, head_local, HD)
        listed_values = value_blocks[group_lists].reshape(members, MOST * BLK, head_local, HD)
        scores = (
            jnp.einsum(
                "gqhd,gkhd->ghqk", group_queries, listed_keys, preferred_element_type=jnp.float32
            )
            * scaling
        )
        usable = (slot_of_key[None, :] < group_counts[:, None])[:, None, None, :]
        largest = jnp.max(jnp.where(usable, scores, -jnp.inf), axis=-1, keepdims=True)
        raised = jnp.where(usable, jnp.exp(scores - largest), 0.0)
        totals = jnp.sum(raised, axis=-1, keepdims=True)
        weights = (raised / totals).astype(jnp.bfloat16)
        output = jnp.einsum(
            "ghqk,gkhd->gqhd", weights, listed_values, preferred_element_type=jnp.float32
        )
        return output.astype(jnp.bfloat16)

    query_blocks = queries.reshape(-1, BLK, queries.shape[1])
    exchanged = lax.all_to_all(query_blocks, "kv", split_axis=2, concat_axis=0, tiled=True)
    block_total = exchanged.shape[0]
    rows = exchanged.shape[1]
    per_group = math.gcd(block_total, max(1, 512 // rows))
    group_total = block_total // per_group
    grouped = exchanged.reshape(group_total, per_group, rows, head_local, HD)
    lists_grouped = key_lists.reshape(group_total, per_group, key_lists.shape[1])
    counts_grouped = counts.reshape(group_total, per_group)
    produced = lax.map(padded_group, (grouped, lists_grouped, counts_grouped))
    joined = produced.reshape(block_total, rows, head_local * HD)
    result = lax.all_to_all(joined, "kv", split_axis=0, concat_axis=2, tiled=True)
    return result.reshape(queries.shape)


def solution(mesh):
    return jax.shard_map(
        per_device,
        mesh=mesh,
        in_specs=(
            P(("pb", "kv"), None),
            P(("pb", "kv"), None),
            P(("pb", "kv"), None),
            P("pb", None),
            P("pb"),
        ),
        out_specs=P(("pb", "kv"), None),
        check_vma=False,
    )
```

profile of v0, /device:TPU:2, one launch (start us, length us, event | category | flops | bytes accessed | tf_op | source)
XLA Modules:
  0.0 411.0 jit_solution(12888155072686574849)
XLA Ops:
  6.5 6.2 %copy.31 = bf16[2,128,4096]{1,0,2:T(2,128)(2,1)} copy(bf16[2,128,4096]{2,1,0:T(8,128)(2,1)} %bitcast.84) | data formatting | bytes 4194304 | tf_op jit(solution)/shard_map/reshape | solution.py:59
  12.7 11.6 %all-to-all-start.1 = ((bf16[2,128,4096]{1,0,2:T(2,128)(2,1)}), bf16[2,128,4096]{1,0,2:T(2,128)(2,1)S(1)}, u32[]{:S(2)}, u32[]{:S(2)}) async-start(bf16[2,128,4096]{1,0,2:T(2,128)(2,1)} %copy.31), calls=%async_computation.1 | async-start | bytes 4194304 | tf_op jit(solution)/shard_map/all_to_all | solution.py:60
  25.1 30.8 %all-gather.5.cloned.1.call-done = bf16[256,4096]{1,0:T(8,128)(2,1)} async-done(((bf16[32,4096]{1,0:T(8,128)(2,1)}), bf16[256,4096]{1,0:T(8,128)(2,1)}) %all-gather.5.cloned.1.call-update) | async-done | bytes 2097168 | tf_op jit(solution)/shard_map/all_gather | solution.py:25
  55.9 4.1 copy.34
  60.0 13.6 %all-to-all-done.1 = bf16[2,128,4096]{1,0,2:T(2,128)(2,1)S(1)} async-done(((bf16[2,128,4096]{1,0,2:T(2,128)(2,1)}), bf16[2,128,4096]{1,0,2:T(2,128)(2,1)S(1)}, u32[]{:S(2)}, u32[]{:S(2)}) %all-to-all-start.1) | async-done | bytes 2097184 | tf_op jit(solution)/shard_map/all_to_all | solution.py:60
  73.6 6.9 %all-to-all-start.2 = ((bf16[256,32,128]{0,2,1:T(8,128)(2,1)}), bf16[256,32,128]{0,2,1:T(8,128)(2,1)}, u32[]{:S(2)}, u32[]{:S(2)}) async-start(bf16[256,32,128]{0,2,1:T(8,128)(2,1)} %bitcast.76), calls=%async_computation.2 | async-start | bytes 4194304 | tf_op jit(solution)/shard_map/all_to_all | solution.py:29
  81.2 30.8 %all-gather.3.cloned.1.call-done = bf16[256,4096]{1,0:T(8,128)(2,1)} async-done(((bf16[32,4096]{1,0:T(8,128)(2,1)}), bf16[256,4096]{1,0:T(8,128)(2,1)}) %all-gather.3.cloned.1.call-update) | async-done | bytes 2097168 | tf_op jit(solution)/shard_map/all_gather | solution.py:26
  112.1 4.1 copy.28
  116.1 12.9 %all-to-all-done.2 = bf16[256,32,128]{0,2,1:T(8,128)(2,1)} async-done(((bf16[256,32,128]{0,2,1:T(8,128)(2,1)}), bf16[256,32,128]{0,2,1:T(8,128)(2,1)}, u32[]{:S(2)}, u32[]{:S(2)}) %all-to-all-start.2) | async-done | bytes 2097184 | tf_op jit(solution)/shard_map/all_to_all | solution.py:29
  129.1 6.7 %all-to-all-start = ((bf16[256,32,128]{0,2,1:T(8,128)(2,1)}), bf16[256,32,128]{0,2,1:T(8,128)(2,1)}, u32[]{:S(2)}, u32[]{:S(2)}) async-start(bf16[256,32,128]{0,2,1:T(8,128)(2,1)} %bitcast.77), calls=%async_computation | async-start | bytes 4194304 | tf_op jit(solution)/shard_map/all_to_all | solution.py:30
  137.7 4.1 copy.33
  141.7 4.1 copy.35
  147.8 37.0 %all-to-all-done = bf16[256,32,128]{0,2,1:T(8,128)(2,1)} async-done(((bf16[256,32,128]{0,2,1:T(8,128)(2,1)}), bf16[256,32,128]{0,2,1:T(8,128)(2,1)}, u32[]{:S(2)}, u32[]{:S(2)}) %all-to-all-start) | async-done | bytes 2097184 | tf_op jit(solution)/shard_map/all_to_all | solution.py:30
  184.8 4.1 copy.29
  188.9 3.4 copy.30
  192.2 154.8 %while.11 = (s32[]{:T(128)}, bf16[16,4,128,1,128]{4,2,1,0,3:T(8,128)(2,1)}, s32[16,4,8]{2,1,0:T(4,128)S(1)}, bf16[64,128,1,128]{3,1,0,2:T(8,128)(2,1)}, s32[16,4...) while((s32[]{:T(128)}, ...), condition=%wide.region_3.4_spmd.clone, body=%wide.region_0.3_spmd.clone.sunk | while | flops 272709728 | bytes 15493133 | solution.py:68
  196.5 2.3 gather_fusion
  206.2 2.3 gather_fusion
  244.9 2.3 gather_fusion
  254.6 2.3 gather_fusion
  264.3 2.3 gather_fusion
  293.3 2.3 gather_fusion
  302.9 2.3 gather_fusion
  347.0 53.5 %all_to_all.62 = bf16[64,128,128]{2,1,0:T(8,128)(2,1)S(1)} all-to-all(bf16[64,128,128]{2,1,0:T(8,128)(2,1)} %bitcast.85), channel_id=1, replica_groups=mesh['pb'=8,'kv'=32] {'kv'}, dimensions={0} | all-to-all | bytes 4194304 | tf_op jit(solution)/shard_map/all_to_all | solution.py:70
  (216 shorter events, 146.6 us)
Async XLA Ops:
  12.7 60.9 %all-to-all-start.1 = ((bf16[2,128,4096]{1,0,2:T(2,128)(2,1)}), bf16[2,128,4096]{1,0,2:T(2,128)(2,1)S(1)}, u32[]{:S(2)}, u32[]{:S(2)}) async-start(bf16[2,128,4096]{1,0,2:T(2,128)(2,1)} %copy.31), calls=%async_computation.1 | async-start | bytes 4194304 | tf_op jit(solution)/shard_map/all_to_all | solution.py:60
  24.3 31.6 %all-gather.5.cloned.1.call-start = ((), (), s32[]{:S(2)}) async-start(), calls=%async_computation.5 | async-start | bytes 2359296 | tf_op jit(solution)/shard_map/all_gather | solution.py:25
  73.6 55.5 %all-to-all-start.2 = ((bf16[256,32,128]{0,2,1:T(8,128)(2,1)}), bf16[256,32,128]{0,2,1:T(8,128)(2,1)}, u32[]{:S(2)}, u32[]{:S(2)}) async-start(bf16[256,32,128]{0,2,1:T(8,128)(2,1)} %bitcast.76), calls=%async_computation.2 | async-start | bytes 4194304 | tf_op jit(solution)/shard_map/all_to_all | solution.py:29
  80.5 31.6 %all-gather.3.cloned.1.call-start = ((), (), s32[]{:S(2)}) async-start(), calls=%async_computation.4 | async-start | bytes 2359296 | tf_op jit(solution)/shard_map/all_gather | solution.py:26
  129.1 6.8 %copy-start = (s32[64,8]{0,1:T(8,128)S(1)}, s32[64,8]{0,1:T(8,128)}, u32[]{:S(2)}) copy-start(s32[64,8]{0,1:T(8,128)} %param.10) | copy-start | bytes 6148
  129.1 6.9 %copy-start.1 = (s32[64]{0:T(128)S(1)}, s32[64]{0:T(128)}, u32[]{:S(2)}) copy-start(s32[64]{0:T(128)} %param.11) | copy-start | bytes 772
  129.1 55.7 %all-to-all-start = ((bf16[256,32,128]{0,2,1:T(8,128)(2,1)}), bf16[256,32,128]{0,2,1:T(8,128)(2,1)}, u32[]{:S(2)}, u32[]{:S(2)}) async-start(bf16[256,32,128]{0,2,1:T(8,128)(2,1)} %bitcast.77), calls=%async_computation | async-start | bytes 4194304 | tf_op jit(solution)/shard_map/all_to_all | solution.py:30
Sparse Core Ops, SparseCore 0:
  27.0 28.8 all-gather.4
  83.2 28.8 all-gather.2
where the time goes:
time: 413 us; the launch traced here: 411 us
  waiting for transfers between devices  127 us (31%)
  local copies, waits for them, and re-layouts  101 us (24%)
  matrix products  56.6 us (14%)
  blocking collectives  53.5 us (13%)
  other arithmetic  33.6 us (8%)
  starting transfers between devices  25.4 us (6%)
  between operations  13.5 us (3%)
    all_to_all x1, blocking collectives, per_device(): lax.all_to_all(joined, 'kv', split_axis=0, concat_axis=2, tiled=True)  53.5 us
    gather x16, local copies, waits for them, and re-layouts, padded_group(): value_blocks[group_lists].reshape(members, MOST * BLK, head_local, HD)  37.4 us
    all_to_all x1, waiting for transfers between devices, per_device(): lax.all_to_all(value_whole, 'kv', split_axis=1, concat_axis=0, tiled=True)  37 us
    dot_general x16, matrix products, padded_group(): jnp.einsum('ghqk,gkhd->gqhd', weights, listed_values, preferred_element_t...  35.1 us
    sub x16, other arithmetic, padded_group(): raised = jnp.where(usable, jnp.exp(scores - largest), 0.0)  32.1 us
    all_gather x1, waiting for transfers between devices, per_device(): lax.all_gather(keys, 'pb', axis=0, tiled=True)  30.8 us
    all_gather x1, waiting for transfers between devices, per_device(): lax.all_gather(values, 'pb', axis=0, tiled=True)  30.8 us
    dot_general x16, matrix products, padded_group(): jnp.einsum('gqhd,gkhd->ghqk', group_queries, listed_keys, preferred_eleme...  21.5 us
  transfers between devices with their start and end apart: 5, of which 5 were waited for; matrix products, arithmetic and copies ran while one was open for 5% of the time, Pallas kernels for 0%

commit v1 on v0

--- a/solution.py
+++ b/solution.py
@@ -1,13 +1,43 @@
+import functools
 import math
 import jax
 import jax.numpy as jnp
 from jax import lax
 from jax.sharding import PartitionSpec as P
+from jax.lax import axis_index, axis_size, ppermute
 
 HEADS = 32
 HD = 128
 BLK = 128
 MOST = 8
+
+
+def try_all_the_vector(block_here, at_axis):
+    current_arr = axis_size("pb")
+    reply, y_new, vec_out = (current_arr, axis_index("pb"), block_here.shape[at_axis])
+    frame_out = jnp.zeros(
+        [j * reply if rr == at_axis else j for rr, j in enumerate(block_here.shape)],
+        block_here.dtype,
+    )
+    part_now = lax.dynamic_update_slice_in_dim(frame_out, block_here, y_new * vec_out, axis=at_axis)
+    local_now = field_out = block_here
+    for k0 in range(1, reply // 2 + 1):
+        local_now = ppermute(
+            local_now, "pb", list(map(lambda rr: (rr, (rr + 1) % reply), range(reply)))
+        )
+        part_now = lax.dynamic_update_slice_in_dim(
+            part_now, local_now, (y_new - k0) % reply * vec_out, axis=at_axis
+        )
+        if 2 * k0 < reply:
+            lower = list(map(lambda rr: (rr, (rr - 1) % reply), range(reply)))
+            field_out = ppermute(field_out, "pb", lower)
+            part_now = lax.dynamic_update_slice_in_dim(
+                part_now, field_out, (y_new + k0) % reply * vec_out, axis=at_axis
+            )
+    return part_now
+
+
+recover_signs = functools.partial(try_all_the_vector, at_axis=0)
 
 
 def regroup(split_array, kv_count, pb_count):
@@ -21,10 +51,7 @@
     pb_count = lax.axis_size("pb")
     head_local = HEADS // kv_count
     scaling = HD ** (-0.5)
-    key_whole, value_whole = (
-        lax.all_gather(keys, "pb", axis=0, tiled=True),
-        lax.all_gather(values, "pb", axis=0, tiled=True),
-    )
+    key_whole, value_whole = (recover_signs(keys), lax.all_gather(values, "pb", axis=0, tiled=True))
     key_split, value_split = (
         lax.all_to_all(key_whole, "kv", split_axis=1, concat_axis=0, tiled=True),
         lax.all_to_all(value_whole, "kv", split_axis=1, concat_axis=0, tiled=True),

time: 413 us -> 492 us (1.19); the launches traced: 411 us -> 483 us
  local copies, waits for them, and re-layouts: 101 us -> 196 us
  waiting for transfers between devices: 127 us -> 90.1 us
  starting transfers between devices: 25.4 us -> 37.5 us
    dynamic_update_slice x0 -> x8, local copies, waits for them, and re-layouts: none -> 88.2 us  [the longest x4 42.6 us: try_all_the_vector(): lax.dynamic_update_slice_in_dim(part_now, local_now, (y_new - k0) % reply...]
    all_gather x1 -> x0, waiting for transfers between devices: 30.8 us -> none  [per_device(): lax.all_gather(keys, 'pb', axis=0, tiled=True)]
    all_to_all x1, waiting for transfers between devices: 13.6 us -> 0.01 us  [per_device(): lax.all_to_all(query_blocks, 'kv', split_axis=2, concat_axis=0, tiled=True)]
    ppermute x0 -> x7, waiting for transfers between devices: none -> 11 us  [the longest x4 10.2 us: try_all_the_vector(): ppermute(local_now, 'pb', list(map(lambda rr: (rr, (rr + 1) % reply), ran...]
    ppermute x0 -> x7, starting transfers between devices: none -> 9.4 us  [the longest x3 9.38 us: try_all_the_vector(): field_out = ppermute(field_out, 'pb', lower)]
    ppermute x0 -> x7, local copies, waits for them, and re-layouts: none -> 8.11 us  [the longest x4 4.79 us: try_all_the_vector(): ppermute(local_now, 'pb', list(map(lambda rr: (rr, (rr + 1) % reply), ran...]
  transfers between devices with their start and end apart: 5 -> 11, of which waited for: 5 -> 7; matrix products, arithmetic and copies ran while one was open for 5% -> 24% of each run, Pallas kernels for 0% -> 0%
where the time goes in v1:
time: 492 us; the launch traced here: 483 us
  local copies, waits for them, and re-layouts  196 us (40%)
  waiting for transfers between devices  90.1 us (18%)
  matrix products  56.6 us (12%)
  blocking collectives  54 us (11%)
  starting transfers between devices  37.5 us (8%)
  other arithmetic  34 us (7%)
  between operations  13.7 us (3%)
    all_to_all x1, blocking collectives, per_device(): lax.all_to_all(joined, 'kv', split_axis=0, concat_axis=2, tiled=True)  54 us
    dynamic_update_slice x4, local copies, waits for them, and re-layouts, try_all_the_vector(): lax.dynamic_update_slice_in_dim(part_now, local_now, (y_new - k0) % reply...  42.6 us
    gather x16, local copies, waits for them, and re-layouts, padded_group(): value_blocks[group_lists].reshape(members, MOST * BLK, head_local, HD)  37.4 us
    dynamic_update_slice x3, local copies, waits for them, and re-layouts, try_all_the_vector(): lax.dynamic_update_slice_in_dim(part_now, field_out, (y_new + k0) % reply...  35.3 us
    all_to_all x1, waiting for transfers between devices, per_device(): lax.all_to_all(value_whole, 'kv', split_axis=1, concat_axis=0, tiled=True)  35.2 us
    dot_general x16, matrix products, padded_group(): jnp.einsum('ghqk,gkhd->gqhd', weights, listed_values, preferred_element_t...  35.1 us
    sub x16, other arithmetic, padded_group(): raised = jnp.where(usable, jnp.exp(scores - largest), 0.0)  32.5 us
    all_gather x1, waiting for transfers between devices, per_device(): lax.all_gather(values, 'pb', axis=0, tiled=True)  30.1 us
  transfers between devices with their start and end apart: 11, of which 7 were waited for; matrix products, arithmetic and copies ran while one was open for 24% of the time, Pallas kernels for 0%

profile of v1, /device:TPU:2, one launch (start us, length us, event | category | flops | bytes accessed | tf_op | source)
XLA Modules:
  0.0 482.8 jit_solution(17842264662182303300)
XLA Ops:
  6.5 6.2 %copy.33 = bf16[2,128,4096]{1,0,2:T(2,128)(2,1)} copy(bf16[2,128,4096]{2,1,0:T(8,128)(2,1)} %bitcast.84) | data formatting | bytes 4194304 | tf_op jit(solution)/shard_map/reshape | solution.py:86
  12.7 11.7 %all-to-all-start.1 = ((bf16[2,128,4096]{1,0,2:T(2,128)(2,1)}), bf16[2,128,4096]{1,0,2:T(2,128)(2,1)S(1)}, u32[]{:S(2)}, u32[]{:S(2)}) async-start(bf16[2,128,4096]{1,0,2:T(2,128)(2,1)} %copy.33), calls=%async_computation.1 | async-start | bytes 4194304 | tf_op jit(solution)/shard_map/all_to_all | solution.py:87
  27.4 4.1 collective-permute-done
  39.3 3.2 collective-permute-start.5
  47.7 10.2 %dynamic_update_slice.28 = bf16[256,4096]{0,1:T(8,128)(2,1)} dynamic-update-slice(bf16[256,4096]{0,1:T(8,128)(2,1)} %broadcast_in_dim.36, bf16[32,4096]{0,1:T(8,128)(2,1)S(1)} %copy.36, s32[]{:T(128)S(6)} %select_n.81, s32[]{:T(128)} %copy.73) | dynamic-update-slice | bytes 524292 | tf_op jit(solution)/shard_map/dynamic_update_slice | solution.py:22
  59.4 11.1 %dynamic_update_slice.29 = bf16[256,4096]{0,1:T(8,128)(2,1)} dynamic-update-slice(bf16[256,4096]{0,1:T(8,128)(2,1)} %dynamic_update_slice.28, bf16[32,4096]{0,1:T(8,128)(2,1)S(1)} %copy.37, s32[]{:T(128)S(6)} %select_n.83, s32[]{:T(128)} %copy.73) | dynamic-update-slice | bytes 524292 | tf_op jit(solution)/shard_map/dynamic_update_slice | solution.py:28
  71.0 11.8 %dynamic_update_slice.30 = bf16[256,4096]{0,1:T(8,128)(2,1)} dynamic-update-slice(bf16[256,4096]{0,1:T(8,128)(2,1)} %dynamic_update_slice.29, bf16[32,4096]{0,1:T(8,128)(2,1)S(1)} %copy.38, s32[]{:T(128)S(6)} %select_n.85, s32[]{:T(128)} %copy.73) | dynamic-update-slice | bytes 524292 | tf_op jit(solution)/shard_map/dynamic_update_slice | solution.py:34
  83.3 11.1 %dynamic_update_slice.31 = bf16[256,4096]{0,1:T(8,128)(2,1)} dynamic-update-slice(bf16[256,4096]{0,1:T(8,128)(2,1)} %dynamic_update_slice.30, bf16[32,4096]{0,1:T(8,128)(2,1)S(1)} %copy.39, s32[]{:T(128)S(6)} %select_n.87, s32[]{:T(128)} %copy.73) | dynamic-update-slice | bytes 524292 | tf_op jit(solution)/shard_map/dynamic_update_slice | solution.py:28
  95.8 11.8 %dynamic_update_slice.32 = bf16[256,4096]{0,1:T(8,128)(2,1)} dynamic-update-slice(bf16[256,4096]{0,1:T(8,128)(2,1)} %dynamic_update_slice.31, bf16[32,4096]{0,1:T(8,128)(2,1)S(1)} %copy.40, s32[]{:T(128)S(6)} %select_n.89, s32[]{:T(128)} %copy.73) | dynamic-update-slice | bytes 524292 | tf_op jit(solution)/shard_map/dynamic_update_slice | solution.py:34
  109.0 11.1 %dynamic_update_slice.33 = bf16[256,4096]{0,1:T(8,128)(2,1)} dynamic-update-slice(bf16[256,4096]{0,1:T(8,128)(2,1)} %dynamic_update_slice.32, bf16[32,4096]{0,1:T(8,128)(2,1)S(1)} %copy.41, s32[]{:T(128)S(6)} %select_n.91, s32[]{:T(128)} %copy.73) | dynamic-update-slice | bytes 524292 | tf_op jit(solution)/shard_map/dynamic_update_slice | solution.py:28
  121.5 11.8 %dynamic_update_slice.34 = bf16[256,4096]{0,1:T(8,128)(2,1)} dynamic-update-slice(bf16[256,4096]{0,1:T(8,128)(2,1)} %dynamic_update_slice.33, bf16[32,4096]{0,1:T(8,128)(2,1)S(1)} %copy.42, s32[]{:T(128)S(6)} %select_n.93, s32[]{:T(128)} %copy.73) | dynamic-update-slice | bytes 524292 | tf_op jit(solution)/shard_map/dynamic_update_slice | solution.py:34
  134.7 9.4 %dynamic_update_slice.35 = bf16[256,4096]{0,1:T(8,128)(2,1)} dynamic-update-slice(bf16[256,4096]{0,1:T(8,128)(2,1)} %dynamic_update_slice.34, bf16[32,4096]{0,1:T(8,128)(2,1)S(1)} %copy.43, s32[]{:T(128)S(6)} %select_n.95, s32[]{:T(128)} %copy.73) | dynamic-update-slice | bytes 524292 | tf_op jit(solution)/shard_map/dynamic_update_slice | solution.py:28
  144.1 9.8 %all-to-all-start.2 = ((bf16[256,32,128]{0,2,1:T(8,128)(2,1)}), bf16[256,32,128]{0,2,1:T(8,128)(2,1)}, u32[]{:S(2)}, u32[]{:S(2)}) async-start(bf16[256,32,128]{0,2,1:T(8,128)(2,1)} %bitcast.77), calls=%async_computation.2 | async-start | bytes 4194304 | tf_op jit(solution)/shard_map/all_to_all | solution.py:56
  154.6 30.1 %all-gather.2.cloned.1.call-done = bf16[256,4096]{1,0:T(8,128)(2,1)} async-done(((bf16[32,4096]{1,0:T(8,128)(2,1)}), bf16[256,4096]{1,0:T(8,128)(2,1)}) %all-gather.2.cloned.1.call-update) | async-done | bytes 2097168 | tf_op jit(solution)/shard_map/all_gather | solution.py:54
  184.7 4.1 copy.30
  188.8 13.2 %all-to-all-done.2 = bf16[256,32,128]{0,2,1:T(8,128)(2,1)} async-done(((bf16[256,32,128]{0,2,1:T(8,128)(2,1)}), bf16[256,32,128]{0,2,1:T(8,128)(2,1)}, u32[]{:S(2)}, u32[]{:S(2)}) %all-to-all-start.2) | async-done | bytes 2097184 | tf_op jit(solution)/shard_map/all_to_all | solution.py:56
  202.0 6.5 %all-to-all-start = ((bf16[256,32,128]{0,2,1:T(8,128)(2,1)}), bf16[256,32,128]{0,2,1:T(8,128)(2,1)}, u32[]{:S(2)}, u32[]{:S(2)}) async-start(bf16[256,32,128]{0,2,1:T(8,128)(2,1)} %bitcast.76), calls=%async_computation | async-start | bytes 4194304 | tf_op jit(solution)/shard_map/all_to_all | solution.py:57
  210.3 4.1 copy.35
  214.4 4.1 copy.44
  220.6 35.2 %all-to-all-done = bf16[256,32,128]{0,2,1:T(8,128)(2,1)} async-done(((bf16[256,32,128]{0,2,1:T(8,128)(2,1)}), bf16[256,32,128]{0,2,1:T(8,128)(2,1)}, u32[]{:S(2)}, u32[]{:S(2)}) %all-to-all-start) | async-done | bytes 2097184 | tf_op jit(solution)/shard_map/all_to_all | solution.py:57
  255.7 4.1 copy.31
  259.8 3.3 copy.32
  263.1 155.1 %while.11 = (s32[]{:T(128)}, bf16[16,4,128,1,128]{4,2,1,0,3:T(8,128)(2,1)}, s32[16,4,8]{2,1,0:T(4,128)S(1)}, bf16[64,128,1,128]{3,1,0,2:T(8,128)(2,1)}, s32[16,4...) while((s32[]{:T(128)}, ...), condition=%wide.region_3.4_spmd.clone, body=%wide.region_0.3_spmd.clone.sunk | while | flops 272709728 | bytes 15493133 | solution.py:95
  418.3 54.0 %all_to_all.62 = bf16[64,128,128]{2,1,0:T(8,128)(2,1)S(1)} all-to-all(bf16[64,128,128]{2,1,0:T(8,128)(2,1)} %bitcast.85), channel_id=1, replica_groups=mesh['pb'=8,'kv'=32] {'kv'}, dimensions={0} | all-to-all | bytes 4194304 | tf_op jit(solution)/shard_map/all_to_all | solution.py:97
  (255 shorter events, 186.6 us)
Async XLA Ops:
  12.7 11.8 %copy-start = (bf16[32,4096]{1,0:T(8,128)(2,1)S(1)}, bf16[32,4096]{1,0:T(8,128)(2,1)}, u32[]{:S(2)}) copy-start(bf16[32,4096]{1,0:T(8,128)(2,1)} %param.8) | copy-start | bytes 786436
  12.7 131.4 %all-to-all-start.1 = ((bf16[2,128,4096]{1,0,2:T(2,128)(2,1)}), bf16[2,128,4096]{1,0,2:T(2,128)(2,1)S(1)}, u32[]{:S(2)}, u32[]{:S(2)}) async-start(bf16[2,128,4096]{1,0,2:T(2,128)(2,1)} %copy.33), calls=%async_computation.1 | async-start | bytes 4194304 | tf_op jit(solution)/shard_map/all_to_all | solution.py:87
  24.5 7.0 %collective-permute-start = (bf16[32,4096]{1,0:T(8,128)(2,1)S(1)}, bf16[32,4096]{1,0:T(8,128)(2,1)S(1)}, u32[]{:S(2)}, u32[]{:S(2)}) collective-permute-start(bf16[32,4096]{1,0:T(8,128)(2,1)S(1)} %copy-done), channel_id=1, source_target_pairs={{0,32},{32,64},{64,96},{96,128},{128,160},{160,192},{192,224},{224... | collective-permute-start | bytes 786440 | tf_op jit(solution)/shard_map/ppermute | solution.py:25
  24.5 7.0 %collective-permute-start.1 = (bf16[32,4096]{1,0:T(8,128)(2,1)S(1)}, bf16[32,4096]{1,0:T(8,128)(2,1)S(1)}, u32[]{:S(2)}, u32[]{:S(2)}) collective-permute-start(bf16[32,4096]{1,0:T(8,128)(2,1)S(1)} %copy-done), channel_id=1, source_target_pairs={{0,224},{32,0},{64,32},{96,64},{128,96},{160,128},{192,160},{224,1... | collective-permute-start | bytes 786440 | tf_op jit(solution)/shard_map/ppermute | solution.py:33
  31.5 14.1 %copy-start.5 = (bf16[32,4096]{1,0:T(8,128)(2,1)}, bf16[32,4096]{1,0:T(8,128)(2,1)S(1)}, u32[]{:S(2)}) copy-start(bf16[32,4096]{1,0:T(8,128)(2,1)S(1)} %collective-permute-done) | copy-start | bytes 786436
  31.5 7.0 %collective-permute-start.2 = (bf16[32,4096]{1,0:T(8,128)(2,1)S(1)}, bf16[32,4096]{1,0:T(8,128)(2,1)S(1)}, u32[]{:S(2)}, u32[]{:S(2)}) collective-permute-start(bf16[32,4096]{1,0:T(8,128)(2,1)S(1)} %collective-permute-done), channel_id=1, source_target_pairs={{0,32},{32,64},{64,96},{96,128},{128,160},{160,192},{192,224},{224... | collective-permute-start | bytes 786440 | tf_op jit(solution)/shard_map/ppermute | solution.py:25
  31.5 0.7 copy-start.1
  32.2 7.1 %collective-permute-start.3 = (bf16[32,4096]{1,0:T(8,128)(2,1)S(1)}, bf16[32,4096]{1,0:T(8,128)(2,1)}, u32[]{:S(2)}, u32[]{:S(2)}) collective-permute-start(bf16[32,4096]{1,0:T(8,128)(2,1)S(1)} %collective-permute-done.1), channel_id=1, source_target_pairs={{0,224},{32,0},{64,32},{96,64},{128,96},{160,128},{192,160},{224,1... | collective-permute-start | bytes 786440 | tf_op jit(solution)/shard_map/ppermute | solution.py:33
  38.5 0.8 copy-start.3
  38.5 7.1 %collective-permute-start.4 = (bf16[32,4096]{1,0:T(8,128)(2,1)S(1)}, bf16[32,4096]{1,0:T(8,128)(2,1)}, u32[]{:S(2)}, u32[]{:S(2)}) collective-permute-start(bf16[32,4096]{1,0:T(8,128)(2,1)S(1)} %collective-permute-done.2), channel_id=1, source_target_pairs={{0,32},{32,64},{64,96},{96,128},{128,160},{160,192},{192,224},{224... | collective-permute-start | bytes 786440 | tf_op jit(solution)/shard_map/ppermute | solution.py:25
  39.3 80.7 %collective-permute-start.5 = (bf16[32,4096]{1,0:T(8,128)(2,1)}, bf16[32,4096]{1,0:T(8,128)(2,1)}, u32[]{:S(2)}, u32[]{:S(2)}) collective-permute-start(bf16[32,4096]{1,0:T(8,128)(2,1)} %collective-permute-done.3), channel_id=1, source_target_pairs={{0,224},{32,0},{64,32},{96,64},{128,96},{160,128},{192,160},{224,1... | collective-permute-start | bytes 786440 | tf_op jit(solution)/shard_map/ppermute | solution.py:33
  45.6 87.6 %collective-permute-start.6 = (bf16[32,4096]{1,0:T(8,128)(2,1)}, bf16[32,4096]{1,0:T(8,128)(2,1)}, u32[]{:S(2)}, u32[]{:S(2)}) collective-permute-start(bf16[32,4096]{1,0:T(8,128)(2,1)} %collective-permute-done.4), channel_id=1, source_target_pairs={{0,32},{32,64},{64,96},{96,128},{128,160},{160,192},{192,224},{224... | collective-permute-start | bytes 786440 | tf_op jit(solution)/shard_map/ppermute | solution.py:25
  58.0 12.5 %copy-start.2 = (bf16[32,4096]{1,0:T(8,128)(2,1)S(1)}, bf16[32,4096]{1,0:T(8,128)(2,1)}, u32[]{:S(2)}) copy-start(bf16[32,4096]{1,0:T(8,128)(2,1)} %copy-done.1) | copy-start | bytes 786436
  71.0 11.8 %copy-start.4 = (bf16[32,4096]{1,0:T(8,128)(2,1)S(1)}, bf16[32,4096]{1,0:T(8,128)(2,1)}, u32[]{:S(2)}) copy-start(bf16[32,4096]{1,0:T(8,128)(2,1)} %copy-done.3) | copy-start | bytes 786436
  144.1 58.0 %all-to-all-start.2 = ((bf16[256,32,128]{0,2,1:T(8,128)(2,1)}), bf16[256,32,128]{0,2,1:T(8,128)(2,1)}, u32[]{:S(2)}, u32[]{:S(2)}) async-start(bf16[256,32,128]{0,2,1:T(8,128)(2,1)} %bitcast.77), calls=%async_computation.2 | async-start | bytes 4194304 | tf_op jit(solution)/shard_map/all_to_all | solution.py:56
  153.9 30.8 %all-gather.2.cloned.1.call-start = ((), (), s32[]{:S(2)}) async-start(), calls=%async_computation.4 | async-start | bytes 2359296 | tf_op jit(solution)/shard_map/all_gather | solution.py:54
  202.0 6.5 %copy-start.6 = (s32[64,8]{0,1:T(8,128)S(1)}, s32[64,8]{0,1:T(8,128)}, u32[]{:S(2)}) copy-start(s32[64,8]{0,1:T(8,128)} %param.10) | copy-start | bytes 6148
  202.0 6.6 %copy-start.7 = (s32[64]{0:T(128)S(1)}, s32[64]{0:T(128)}, u32[]{:S(2)}) copy-start(s32[64]{0:T(128)} %param.11) | copy-start | bytes 772
  202.0 53.7 %all-to-all-start = ((bf16[256,32,128]{0,2,1:T(8,128)(2,1)}), bf16[256,32,128]{0,2,1:T(8,128)(2,1)}, u32[]{:S(2)}, u32[]{:S(2)}) async-start(bf16[256,32,128]{0,2,1:T(8,128)(2,1)} %bitcast.76), calls=%async_computation | async-start | bytes 4194304 | tf_op jit(solution)/shard_map/all_to_all | solution.py:57
Sparse Core Ops, SparseCore 0:
  156.6 28.0 all-gather.1
